TPU v7x, 128 devices: a whole 4x4x4 slice. The times are simulated.
128 devices in a mesh: req: 16 (over z, x), tp: 8 (over y, core).
Axes of the slice: x: 4, y: 4, z: 4, core: 2. Of those that a mesh axis runs over, the one named last changes fastest.
Arguments:
- tokens: bfloat16 [8192, 3072], P('req', 'tp'), may hold values from -3 to 3
- norm_gain: bfloat16 [3072], P('tp'), may hold values from 0.099609375 to 1.8984375
- w_query: bfloat16 [3072, 3072], P(None, 'tp'), may hold values from -0.3125 to 0.3125
- w_key: bfloat16 [3072, 3072], P(None, 'tp'), may hold values from -0.109375 to 0.109375
- w_value: bfloat16 [3072, 3072], P(None, 'tp'), may hold values from -0.109375 to 0.109375
- w_out: bfloat16 [3072, 3072], P('tp'), may hold values from -0.109375 to 0.109375
- prev_keys: bfloat16 [65536, 3072], P('req', 'tp'), may hold values from -300 to 300
- prev_values: bfloat16 [65536, 3072], P('req', 'tp'), may hold values from -6 to 6
- earlier_lengths: int32 [16, 4], P('req'), may hold values from 1 to 2048, 4096 in all within a row
- new_lengths: int32 [16, 4], P('req'), may hold values from 1 to 256, 512 in all within a row
- page_table: int32 [16, 36], P('req'), may hold values from 0 to 575, as said below
Outputs:
- layer_out: bfloat16 [8192, 3072], P('req', 'tp')
- decode_pool: bfloat16 [288, 8, 128, 1536], P('req', 'tp')
Inputs may be any that keep to these rules, and one draw needn't show every extreme that they name: `page_table`: every value appears exactly once. Among the pages of one index of req, at most 2 share the same value // 18, and in every draw some destination receives exactly 2 of them.
All inputs are finite; a program needn't handle non-finite values.
Results may differ from a plain program's by a relative error of at most 0.0075.
Values may be sent and summed in bfloat16 or wider, within the bound.
No kernel may reach another device: no remote copies, remote signals or barrier semaphores. Data moves between devices by JAX's collectives and lax.ppermute only.
A program may use at most 256 MiB of HBM per device.

v0:
```python
import math
import jax
import jax.numpy as jnp
from jax import lax
from jax.sharding import PartitionSpec as P

HD = 96
HG = 4
PAGE = 128
EPSILON = 1e-05
THETA = 10000.0


def from_partner(value, axis, distance):
    mask = 2**distance
    pairs = [(source, source ^ mask) for source in range(lax.axis_size(axis))]
    return lax.ppermute(value, axis, pairs)


def rotate(values, positions, head_size):
    count = values.shape[0]
    half_size = head_size // 2
    shaped = values.reshape(count, -1, head_size)
    freqs = jnp.exp(-math.log(THETA) * 2.0 * jnp.arange(half_size, dtype=jnp.float32) / head_size)
    angles = positions.astype(jnp.float32)[:, None] * freqs[None, :]
    cosine = jnp.cos(angles)[:, None, :]
    sine = jnp.sin(angles)[:, None, :]
    first = shaped[:, :, :half_size]
    second = shaped[:, :, half_size:]
    turned = jnp.concatenate(
        [first * cosine - second * sine, second * cosine + first * sine], axis=2
    )
    return turned.reshape(count, -1)


def request_ids(lengths, count):
    ends = jnp.cumsum(lengths)
    row_index = jnp.arange(count, dtype=jnp.int32)
    return jnp.sum((row_index[:, None] >= ends[None, :]).astype(jnp.int32), axis=1)


def block_layout(earlier, fresh, count):
    owners = request_ids(fresh, count)
    starts = jnp.cumsum(fresh) - fresh
    onehot = (owners[:, None] == jnp.arange(fresh.shape[0], dtype=jnp.int32)[None, :]).astype(
        jnp.int32
    )
    first_row = jnp.sum(onehot * starts[None, :], axis=1)
    before = jnp.sum(onehot * earlier[None, :], axis=1)
    row_index = jnp.arange(count, dtype=jnp.int32)
    return (owners, before + row_index - first_row)


def visible(earlier, owners, prev_count, count):
    prev_owner = request_ids(earlier, prev_count)
    row_index = jnp.arange(count, dtype=jnp.int32)
    old_part = owners[:, None] == prev_owner[None, :]
    new_part = (owners[:, None] == owners[None, :]) & (row_index[None, :] <= row_index[:, None])
    return jnp.concatenate([old_part, new_part], axis=1)


def order_pair(mine, partner, own_half):
    lower = jnp.where(own_half == 0, mine, partner)
    upper = jnp.where(own_half == 0, partner, mine)
    return jnp.stack([lower, upper], axis=1)


def join_heads(stacked, local_width):
    count, halves, rows_page = (stacked.shape[0], stacked.shape[1], stacked.shape[2])
    split_rows = stacked.reshape(count, halves, rows_page, 2, local_width)
    return split_rows.transpose(0, 2, 3, 1, 4).reshape(count, rows_page, 2 * halves * local_width)


def fill_pool(page_rows, slot_ids, slot_count):
    empty = jnp.zeros((slot_count + 1, page_rows.shape[1], page_rows.shape[2]), jnp.bfloat16)
    return empty.at[slot_ids].set(page_rows)[:slot_count][:, None]


def shards(
    tokens,
    norm_gain,
    w_query,
    w_key,
    w_value,
    w_out,
    prev_keys,
    prev_values,
    earlier_lengths,
    new_lengths,
    page_table,
):
    token_count, local_width = tokens.shape
    full_width = w_query.shape[0]
    widened = tokens.astype(jnp.float32)
    square_sums = lax.psum(jnp.sum(widened * widened, axis=1), "tp")
    scaling = lax.rsqrt(square_sums / full_width + EPSILON)
    normed = (widened * scaling[:, None] * norm_gain.astype(jnp.float32)[None, :]).astype(
        jnp.bfloat16
    )
    fragment = lax.all_gather(normed, "tp", axis=1, tiled=True)
    query_raw, key_raw, value_raw = tuple(
        (
            jnp.dot(fragment, weight, preferred_element_type=jnp.float32)
            for weight in (w_query, w_key, w_value)
        )
    )
    earlier = earlier_lengths[0]
    fresh = new_lengths[0]
    owners, positions = block_layout(earlier, fresh, token_count)
    queries = rotate(query_raw, positions, HD).astype(jnp.bfloat16)
    new_keys = rotate(key_raw, positions, HD).astype(jnp.bfloat16)
    new_values = value_raw.astype(jnp.bfloat16)
    keys_all = jnp.concatenate([prev_keys, new_keys], axis=0)
    values_all = jnp.concatenate([prev_values, new_values], axis=0)
    allowed = visible(earlier, owners, prev_keys.shape[0], token_count)
    heads_here = local_width // HD
    scores = jnp.einsum(
        "qhd,khd->hqk",
        queries.reshape(token_count, heads_here, HD),
        keys_all.reshape(-1, heads_here, HD),
        preferred_element_type=jnp.float32,
    ) * HD ** (-0.5)
    scores = jnp.where(allowed[None, :, :], scores, -1e30)
    row_peak = jnp.max(scores, axis=2, keepdims=True)
    weights = jnp.exp(scores - row_peak)
    totals = jnp.sum(weights, axis=2)
    prob_rows = weights.astype(jnp.bfloat16)
    mixture = jnp.einsum(
        "hqk,khd->qhd",
        prob_rows,
        values_all.reshape(-1, heads_here, HD),
        preferred_element_type=jnp.float32,
    )
    attended = (
        (mixture / totals.T[:, :, None]).astype(jnp.bfloat16).reshape(token_count, local_width)
    )
    projected = jnp.dot(attended, w_out, preferred_element_type=jnp.float32)
    summed = lax.psum_scatter(projected, "tp", scatter_dimension=1, tiled=True)
    layer_out = (tokens.astype(jnp.float32) + summed).astype(jnp.bfloat16)
    page_total = keys_all.shape[0] // PAGE
    page_rows = jnp.concatenate(
        [
            keys_all.reshape(page_total, PAGE, local_width),
            values_all.reshape(page_total, PAGE, local_width),
        ],
        axis=2,
    )
    req_count = lax.axis_size("req")
    halves = lax.axis_size("tp") // HG
    slot_count = page_total // halves
    dest_count = req_count * halves
    capacity = 2 * ((page_total // 2 + dest_count - 1) // dest_count)
    table = page_table[0]
    target = table // slot_count
    slot_ids = table % slot_count
    own_half = lax.axis_index("tp") % halves
    order_index = jnp.arange(page_total, dtype=jnp.int32)
    earlier_mask = order_index[:, None] > order_index[None, :]
    placing = jnp.sum(
        ((target[:, None] == target[None, :]) & earlier_mask).astype(jnp.int32), axis=1
    )
    bucket = target * capacity + placing
    send_rows = (
        jnp.zeros((dest_count * capacity, PAGE, 2 * local_width), jnp.bfloat16)
        .at[bucket]
        .set(page_rows)
    )
    send_slots = jnp.full((dest_count * capacity,), slot_count, jnp.int32).at[bucket].set(slot_ids)
    got_rows, got_slots = (
        lax.all_to_all(send_rows, "req", split_axis=0, concat_axis=0, tiled=True),
        lax.all_to_all(send_slots, "req", split_axis=0, concat_axis=0, tiled=True),
    )
    got_rows = got_rows.reshape(req_count, halves, capacity, PAGE, 2 * local_width)
    got_slots = got_slots.reshape(req_count, halves, capacity)
    mine = lax.dynamic_index_in_dim(got_rows, own_half, 1, keepdims=False).reshape(
        req_count * capacity, PAGE, 2 * local_width
    )
    final_slots = lax.dynamic_index_in_dim(got_slots, own_half, 1, keepdims=False).reshape(-1)
    other = lax.dynamic_index_in_dim(got_rows, 1 - own_half, 1, keepdims=False).reshape(
        req_count * capacity, PAGE, 2 * local_width
    )
    partner = from_partner(other, "tp", 0)
    stacked = order_pair(mine, partner, own_half)
    final_rows = join_heads(stacked, local_width)
    decode_pool = fill_pool(final_rows, final_slots, slot_count)
    return (layer_out, decode_pool)


def solution(mesh):
    placed = (
        P("req", "tp"),
        P("tp"),
        P(None, "tp"),
        P(None, "tp"),
        P(None, "tp"),
        P("tp", None),
        P("req", "tp"),
        P("req", "tp"),
        P("req", None),
        P("req", None),
        P("req", None),
    )
    return jax.shard_map(
        shards,
        mesh=mesh,
        in_specs=placed,
        out_specs=(P("req", "tp"), P("req", "tp", None, None)),
        check_vma=False,
    )
```

profile of v0, /device:TPU:1, one launch (start us, length us, event | category | flops | bytes accessed | tf_op | source)
XLA Modules:
  0.0 441.5 jit_solution(15881802135246873474)
XLA Ops:
  7.2 0.8 convert_element_type.47
  8.1 1.1 fusion.16
  9.2 13.5 %psum.7 = f32[512]{0:T(512)S(1)} all-reduce(f32[512]{0:T(512)S(1)} %fusion.16), channel_id=1, replica_groups=mesh['req'=16,'tp'=8] {'tp'}, use_global_device_ids=true, to_apply=%region_1.0 | all-reduce | flops 512 | bytes 4096 | tf_op jit(solution)/shard_map/psum | solution.py:95
  22.7 1.9 fusion.18
  24.6 0.8 reduce-window.13
  25.4 0.8 reduce-window.14
  26.4 0.7 fusion.25
  27.0 0.7 fusion.26
  28.0 0.7 fusion.31
  28.7 0.7 select_reduce_fusion.1
  29.4 0.7 fusion.29
  30.1 0.4 multiply_cosine_fusion
  30.7 1.3 broadcast_compare_fusion
  32.0 1.6 pad_add_fusion
  33.6 21.3 %all-gather.2.cloned.1.call-done = bf16[512,3072]{1,0:T(8,128)(2,1)} async-done(((bf16[512,384]{1,0:T(8,128)(2,1)}), bf16[512,3072]{1,0:T(8,128)(2,1)}) %all-gather.2.cloned.1.call-update) | async-done | bytes 3145744 | tf_op jit(solution)/shard_map/all_gather | solution.py:100
  54.9 4.2 fusion.38
  59.2 1.4 fusion.37
  60.6 0.3 subtract_convert_fusion.1
  61.1 4.0 pad_maximum_fusion.2
  65.1 5.8 %copy.54 = bf16[4608,384]{0,1:T(8,128)(2,1)} copy(bf16[4608,384]{1,0:T(8,128)(2,1)} %pad_maximum_fusion.2) | data formatting | bytes 7077888 | tf_op jit(solution)/shard_map/concatenate | solution.py:113
  70.9 4.5 %convolution_convert_fusion = bf16[512,384]{1,0:T(8,128)(2,1)S(1)} fusion(bf16[512,3072]{1,0:T(8,128)(2,1)} %all-gather.2.cloned.1.call-done, bf16[3072,384]{1,0:T(8,128)(2,1)} %param.15), kind=kOutput, calls=%fused_computation.20 | convolution fusion | flops 1208156160 | bytes 5898240 | tf_op jit(solution)/shard_map/dot_general | solution.py:103
  75.4 0.4 pad_maximum_fusion.1
  75.8 7.1 %pad_maximum_fusion = bf16[36,128,768]{2,1,0:T(8,128)(2,1)} fusion(bf16[36,128,384]{2,1,0:T(8,128)(2,1)S(1)} %bitcast.89, bf16[36,128,384]{2,1,0:T(8,128)(2,1)} %bitcast.90), kind=kLoop, calls=%fused_computation.13 | loop fusion | flops 14155776 | bytes 14155776 | tf_op jit(solution)/shard_map/concatenate | solution.py:141
  82.9 6.0 %broadcast_in_dim.20 = bf16[64,128,768]{2,1,0:T(8,128)(2,1)} broadcast(bf16[]{:T(256)} %constant.76.clone.1), dimensions={} | broadcast | bytes 12582914 | tf_op jit(solution)/shard_map/broadcast_in_dim | solution.py:164
  88.9 22.5 %scatter_fusion = bf16[64,128,768]{2,1,0:T(8,128)(2,1)} fusion(bf16[64,128,768]{2,1,0:T(8,128)(2,1)} %broadcast_in_dim.20, s32[36]{0:T(128)S(1)} %fusion.29, bf16[36,128,768]{2,1,0:T(8,128)(2,1)} %pad_maximum_fusion), kind=kCustom, calls=%fused_computation.1 | custom fusion | bytes 21233808 | tf_op jit(solution)/shard_map/scatter | solution.py:166
  111.4 6.7 %all-to-all-start.1 = ((bf16[64,128,768]{2,1,0:T(8,128)(2,1)}), bf16[64,128,768]{2,1,0:T(8,128)(2,1)}, u32[]{:S(2)}, u32[]{:S(2)}) async-start(bf16[64,128,768]{2,1,0:T(8,128)(2,1)} %scatter_fusion), calls=%async_computation.2 | async-start | bytes 25165824 | tf_op jit(solution)/shard_map/all_to_all | solution.py:170
  118.3 18.6 %fusion = (f32[4,512]{1,0:T(4,128)S(1)}, f32[4,512,4608]{2,1,0:T(8,128)}) fusion(pred[512,4608]{1,0:T(8,128)(4,1)} %pad_add_fusion, bf16[4608,4,96]{0,2,1:T(8,128)(2,1)} %bitcast.94, bf16[512,4,48]{0,2,1:T(8,128)(2,1)S(1)} %get-tuple-element.17, bf16[512,4,48]{0,2,1:T(8,128)(2,1)S(1)} %get-tuple-element.16), kind=kOutput, calls=%fused_computation.5 | convolution fusion | flops 1841035264 | bytes 44048384 | tf_op jit(solution)/shard_map/qhd,khd->hqk/dot_general | solution.py:117
  136.8 5.7 %copy.52 = bf16[4608,384]{0,1:T(8,128)(2,1)} copy(bf16[4608,384]{1,0:T(8,128)(2,1)} %copy-done.1) | data formatting | bytes 7077888 | tf_op jit(solution)/shard_map/concatenate | solution.py:114
  142.6 18.2 %fusion.1 = f32[4,512]{1,0:T(4,128)S(1)} fusion(f32[4,512,4608]{2,1,0:T(8,128)} %get-tuple-element.26, f32[4,512]{1,0:T(4,128)S(1)} %get-tuple-element.25, pred[512,4608]{1,0:T(8,128)(4,1)} %pad_add_fusion), kind=kLoop, calls=%fused_computation.6 | loop fusion | flops 37746688 | bytes 40124416 | tf_op jit(solution)/shard_map/reduce_sum | solution.py:126
  160.8 15.3 %fusion.12 = bf16[512,4,96]{0,2,1:T(8,128)(2,1)S(1)} fusion(bf16[4608,4,96]{0,2,1:T(8,128)(2,1)S(1)} %bitcast.95, f32[4,512,4608]{2,1,0:T(8,128)} %get-tuple-element.26, f32[4,512]{1,0:T(4,128)S(1)} %get-tuple-element.25, pred[512,4608]{1,0:T(8,128)(4,1)S(1)} %copy-done.2, f32[512,4]{0,1:T(4,128)S(1)} %bitcast.100), kind=kOutput, calls=%fused_computation.25 | convolution fusion | flops 1850081280 | bytes 44056576 | tf_op jit(solution)/shard_map/hqk,khd->qhd/dot_general | solution.py:128
  176.2 4.5 %fusion.39 = f32[512,3072]{1,0:T(8,128)} fusion(bf16[512,384]{0,1:T(8,128)(2,1)S(1)} %bitcast.99, bf16[384,3072]{1,0:T(8,128)(2,1)S(1)} %copy-done), kind=kOutput, calls=%fused_computation.83 | convolution fusion | flops 1207959552 | bytes 9043968 | tf_op jit(solution)/shard_map/dot_general | solution.py:137
  180.7 125.3 %all-to-all-done.1 = bf16[64,128,768]{2,1,0:T(8,128)(2,1)} async-done(((bf16[64,128,768]{2,1,0:T(8,128)(2,1)}), bf16[64,128,768]{2,1,0:T(8,128)(2,1)}, u32[]{:S(2)}, u32[]{:S(2)}) %all-to-all-start.1) | async-done | bytes 12582944 | tf_op jit(solution)/shard_map/all_to_all | solution.py:170
  306.0 10.7 %constant_dynamic-slice_fusion = (bf16[16,1,2,128,768]{4,3,2,1,0:T(8,128)(2,1)}, bf16[16,1,2,128,768]{4,3,2,1,0:T(8,128)(2,1)}) fusion(bf16[16,2,2,128,768]{4,3,2,1,0:T(8,128)(2,1)} %bitcast.28, s32[]{:T(128)S(6)} %select_n.86, s32[]{:T(128)S(6)} %select_n.89), kind=kLoop, calls=%fused_computation.63 | loop fusion | bytes 25165832 | tf_op jit(solution)/shard_map/jit(dynamic_index_in_dim)/dynamic_slice | solution.py:175
  316.7 1.4 collective-permute-start
  318.1 0.7 scatter_custom_fusion
  318.8 0.7 all_to_all.9
  319.5 3.7 all-to-all-start
  323.2 6.0 %all-to-all-done = s32[16,4,1]{1,2,0:T(1,128)S(1)} async-done(((s32[16,4,1]{1,2,0:T(1,128)}), s32[16,4,1]{1,2,0:T(1,128)S(1)}, u32[]{:S(2)}, u32[]{:S(2)}) %all-to-all-start) | async-done | bytes 288 | tf_op jit(solution)/shard_map/all_to_all | solution.py:171
  329.5 2.0 fusion.19
  331.5 10.3 %bitcast_select_fusion.1 = (bf16[32,128,768]{2,1,0:T(8,128)(2,1)}, bf16[32,128,768]{2,1,0:T(8,128)(2,1)}) fusion(bf16[32,128,768]{2,1,0:T(8,128)(2,1)} %collective-permute-done, bf16[16,1,2,128,768]{4,3,2,1,0:T(8,128)(2,1)} %get-tuple-element.14, pred[]{:T(512)S(6)} %eq.75), kind=kLoop, calls=%fused_computation.15 | loop fusion | flops 6291456 | bytes 25165824 | tf_op jit(solution)/shard_map/jit(_where)/select_n | solution.py:63
  341.8 8.7 %copy.58 = bf16[32,128,768]{1,2,0:T(8,128)(2,1)} copy(bf16[32,128,768]{2,1,0:T(8,128)(2,1)} %get-tuple-element.12) | data formatting | bytes 12582912 | tf_op jit(solution)/shard_map/jit(_where)/select_n | solution.py:63
  350.5 8.6 %copy.59 = bf16[32,128,768]{1,2,0:T(8,128)(2,1)} copy(bf16[32,128,768]{2,1,0:T(8,128)(2,1)} %get-tuple-element.13) | data formatting | bytes 12582912 | tf_op jit(solution)/shard_map/jit(_where)/select_n | solution.py:64
  359.1 6.2 %maximum_bitcast_fusion = bf16[32,128,2,2,384]{1,4,2,0,3:T(8,128)(2,1)S(1)} fusion(bf16[32,1,128,2,384]{2,4,3,0,1:T(8,128)(2,1)} %bitcast.92, bf16[32,1,128,2,384]{2,4,3,0,1:T(8,128)(2,1)} %bitcast.91), kind=kLoop, calls=%fused_computation.10 | loop fusion | flops 6291456 | bytes 25165824 | tf_op jit(solution)/shard_map/transpose | solution.py:71
  365.3 5.7 %copy.60 = bf16[32,128,2,2,384]{1,4,3,2,0:T(8,128)(2,1)} copy(bf16[32,128,2,2,384]{1,4,2,0,3:T(8,128)(2,1)S(1)} %maximum_bitcast_fusion) | data formatting | bytes 25165824 | tf_op jit(solution)/shard_map/transpose | solution.py:71
  371.0 16.6 %copy.61 = bf16[32,128,1536]{2,1,0:T(8,128)(2,1)} copy(bf16[32,128,1536]{1,2,0:T(8,128)(2,1)} %bitcast.88) | data formatting | bytes 25165824 | tf_op jit(solution)/shard_map/reshape | solution.py:71
  387.6 3.7 broadcast_in_dim.18
  391.4 36.8 %scatter_fusion.1 = bf16[19,128,1536]{2,1,0:T(8,128)(2,1)} fusion(bf16[19,128,1536]{2,1,0:T(8,128)(2,1)} %broadcast_in_dim.18, s32[32]{0:T(128)S(1)} %fusion.30, bf16[32,128,1536]{2,1,0:T(8,128)(2,1)} %copy.61), kind=kCustom, calls=%fused_computation.2 | custom fusion | bytes 37748864 | tf_op jit(solution)/shard_map/scatter | solution.py:76
  428.1 6.6 %slice_bitcast_fusion = bf16[18,1,128,1536]{3,2,1,0:T(8,128)(2,1)} fusion(bf16[19,128,1536]{2,1,0:T(8,128)(2,1)} %scatter_fusion.1), kind=kLoop, calls=%fused_computation.12 | loop fusion | bytes 14155776
  (36 shorter events, 1.5 us)
Async XLA Ops:
  7.2 169.0 %copy-start = (bf16[384,3072]{1,0:T(8,128)(2,1)S(1)}, bf16[384,3072]{1,0:T(8,128)(2,1)}, u32[]{:S(2)}) copy-start(bf16[384,3072]{1,0:T(8,128)(2,1)} %param.16) | copy-start | bytes 7077892
  7.2 47.7 %all-gather.2.cloned.1.call-start = ((), (), s32[]{:S(2)}) async-start(), calls=%async_computation.3 | async-start | bytes 3538944 | tf_op jit(solution)/shard_map/all_gather | solution.py:100
  54.9 4.2 copy-start.6
  54.9 4.3 copy-start.7
  70.9 4.6 %copy-start.5 = (bf16[4096,384]{1,0:T(8,128)(2,1)S(1)}, bf16[4096,384]{1,0:T(8,128)(2,1)}, u32[]{:S(2)}) copy-start(bf16[4096,384]{1,0:T(8,128)(2,1)} %param.18) | copy-start | bytes 9437188
  75.8 7.1 %copy-start.1 = (bf16[4608,384]{1,0:T(8,128)(2,1)}, bf16[4608,384]{1,0:T(8,128)(2,1)S(1)}, u32[]{:S(2)}) copy-start(bf16[4608,384]{1,0:T(8,128)(2,1)S(1)} %pad_maximum_fusion.1) | copy-start | bytes 10616836
  111.4 194.7 %all-to-all-start.1 = ((bf16[64,128,768]{2,1,0:T(8,128)(2,1)}), bf16[64,128,768]{2,1,0:T(8,128)(2,1)}, u32[]{:S(2)}, u32[]{:S(2)}) async-start(bf16[64,128,768]{2,1,0:T(8,128)(2,1)} %scatter_fusion), calls=%async_computation.2 | async-start | bytes 25165824 | tf_op jit(solution)/shard_map/all_to_all | solution.py:170
  118.0 211.5 %reduce-scatter.2.cloned.1.call-start = ((), (), s32[]{:S(2)}) async-start(), calls=%async_computation.4 | async-start | bytes 7077888 | tf_op jit(solution)/shard_map/reduce_scatter | solution.py:138
  142.6 18.2 %copy-start.2 = (pred[512,4608]{1,0:T(8,128)(4,1)S(1)}, pred[512,4608]{1,0:T(8,128)(4,1)}, u32[]{:S(2)}) copy-start(pred[512,4608]{1,0:T(8,128)(4,1)} %pad_add_fusion) | copy-start | bytes 7077892
  142.6 18.2 %copy-start.3 = (bf16[4608,384]{0,1:T(8,128)(2,1)S(1)}, bf16[4608,384]{0,1:T(8,128)(2,1)}, u32[]{:S(2)}) copy-start(bf16[4608,384]{0,1:T(8,128)(2,1)} %copy.52) | copy-start | bytes 10616836
  306.0 23.5 %copy-start.4 = (bf16[512,384]{1,0:T(8,128)(2,1)S(1)}, bf16[512,384]{1,0:T(8,128)(2,1)}, u32[]{:S(2)}) copy-start(bf16[512,384]{1,0:T(8,128)(2,1)} %param.11) | copy-start | bytes 1179652
  316.7 14.8 %collective-permute-start = (bf16[32,128,768]{2,1,0:T(8,128)(2,1)}, bf16[32,128,768]{2,1,0:T(8,128)(2,1)}, u32[]{:S(2)}, u32[]{:S(2)}) collective-permute-start(bf16[32,128,768]{2,1,0:T(8,128)(2,1)} %bitcast.93), channel_id=1, source_target_pairs={{0,1},{1,0},{2,3},{3,2},{4,5},{5,4},{6,7},{7,6},{8,9},{9,8},{10,11... | collective-permute-start | bytes 18874376 | tf_op jit(solution)/shard_map/ppermute | solution.py:17
  319.5 9.7 %all-to-all-start = ((s32[16,4,1]{1,2,0:T(1,128)}), s32[16,4,1]{1,2,0:T(1,128)S(1)}, u32[]{:S(2)}, u32[]{:S(2)}) async-start(s32[16,4,1]{1,2,0:T(1,128)} %bitcast.23), calls=%async_computation.1 | async-start | bytes 16384 | tf_op jit(solution)/shard_map/all_to_all | solution.py:171
Sparse Core Ops, SparseCore 0:
  24.7 30.1 all-gather.1
  180.8 41.9 reduce-scatter.1
where the time goes:
time: 444 us; the launch traced here: 442 us
  waiting for transfers between devices  153 us (34%)
  local copies, waits for them, and re-layouts  139 us (31%)
  other arithmetic  61.3 us (14%)
  matrix products  48.6 us (11%)
  between operations  14.3 us (3%)
  blocking collectives  13.5 us (3%)
  starting transfers between devices  12 us (3%)
    all_to_all x1, waiting for transfers between devices, shards(): lax.all_to_all(send_rows, 'req', split_axis=0, concat_axis=0, tiled=True)  125 us
    scatter x1, local copies, waits for them, and re-layouts, fill_pool(): return empty.at[slot_ids].set(page_rows)[:slot_count][:, None]  36.8 us
    scatter x1, local copies, waits for them, and re-layouts, shards(): send_rows = jnp.zeros((dest_count * capacity, PAGE, 2 * local_width), jnp...  22.5 us
    all_gather x1, waiting for transfers between devices, shards(): fragment = lax.all_gather(normed, 'tp', axis=1, tiled=True)  21.3 us
    dot_general x1, matrix products, shards(): jnp.einsum('qhd,khd->hqk', queries.reshape(token_count, heads_here, HD),...  18.6 us
    reduce_sum x1, other arithmetic, shards(): totals = jnp.sum(weights, axis=2)  18.2 us
    reshape x1, local copies, waits for them, and re-layouts, join_heads(): split_rows.transpose(0, 2, 3, 1, 4)  16.6 us
    dot_general x1, matrix products, shards(): jnp.einsum('hqk,khd->qhd', prob_rows, values_all.reshape(-1, heads_here,...  15.3 us
  transfers between devices with their start and end apart: 5, of which 3 were waited for; matrix products, arithmetic and copies ran while one was open for 19% of the time, Pallas kernels for 0%

commit v1 on v0

--- a/solution.py
+++ b/solution.py
@@ -9,6 +9,32 @@
 PAGE = 128
 EPSILON = 1e-05
 THETA = 10000.0
+
+
+def sample_post(unit, in_dim, named_axis="tp"):
+    n_lanes = jax.lax.axis_size(named_axis)
+    seen = []
+    h = 0
+    while h < n_lanes:
+        seen.append((h, (h + 1) % n_lanes))
+        h = h + 1
+    rows = []
+    h = 0
+    while h < n_lanes:
+        rows.append((h, (h - 1) % n_lanes))
+        h = h + 1
+    latest, r2 = ([unit], [unit])
+    for _ in range(n_lanes // 2):
+        finding = jax.lax.ppermute(latest[-1], named_axis, seen)
+        latest.append(finding)
+    dev_j = 0
+    while dev_j < (n_lanes - 1) // 2:
+        r2.append(jax.lax.ppermute(r2[-1], named_axis, rows))
+        dev_j += 1
+    piece_next = jnp.concatenate([*latest[::-1], *r2[1:]], axis=in_dim)
+    m_next = jax.lax.axis_index(named_axis)
+    outer = jnp.roll(piece_next, (m_next - n_lanes // 2) * unit.shape[in_dim], axis=in_dim)
+    return outer
 
 
 def from_partner(value, axis, distance):
@@ -97,7 +123,7 @@
     normed = (widened * scaling[:, None] * norm_gain.astype(jnp.float32)[None, :]).astype(
         jnp.bfloat16
     )
-    fragment = lax.all_gather(normed, "tp", axis=1, tiled=True)
+    fragment = sample_post(normed, 1)
     query_raw, key_raw, value_raw = tuple(
         (
             jnp.dot(fragment, weight, preferred_element_type=jnp.float32)

time: 444 us -> 450 us (1.014)
  waiting for transfers between devices: 153 us -> 122 us
  starting transfers between devices: 12 us -> 39.6 us
  local copies, waits for them, and re-layouts: 139 us -> 150 us
    all_gather x1 -> x0, waiting for transfers between devices: 21.3 us -> none  [shards(): fragment = lax.all_gather(normed, 'tp', axis=1, tiled=True)]
    all_to_all x1, waiting for transfers between devices: 125 us -> 108 us  [shards(): lax.all_to_all(send_rows, 'req', split_axis=0, concat_axis=0, tiled=True)]
    ppermute x0 -> x7, starting transfers between devices: none -> 16.8 us  [the longest x3 9.32 us: sample_post(): r2.append(jax.lax.ppermute(r2[-1], named_axis, rows))]
    unnamed x17 -> x46, local copies, waits for them, and re-layouts: 6.66 us -> 16.9 us
    ppermute x0 -> x7, waiting for transfers between devices: none -> 7.75 us  [the longest x4 7.64 us: sample_post(): finding = jax.lax.ppermute(latest[-1], named_axis, seen)]
    ppermute x1, starting transfers between devices: 1.36 us -> 8.51 us  [from_partner(): return lax.ppermute(value, axis, pairs)]
  transfers between devices with their start and end apart: 5 -> 11, of which waited for: 3 -> 7; matrix products, arithmetic and copies ran while one was open for 19% -> 20% of each run, Pallas kernels for 0% -> 0%
where the time goes in v1:
time: 450 us; the launch traced here: 446 us
  local copies, waits for them, and re-layouts  150 us (33%)
  waiting for transfers between devices  122 us (27%)
  other arithmetic  61.3 us (14%)
  matrix products  44.9 us (10%)
  starting transfers between devices  39.6 us (9%)
  between operations  14.5 us (3%)
  blocking collectives  13.5 us (3%)
    all_to_all x1, waiting for transfers between devices, shards(): lax.all_to_all(send_rows, 'req', split_axis=0, concat_axis=0, tiled=True)  108 us
    scatter x1, local copies, waits for them, and re-layouts, fill_pool(): return empty.at[slot_ids].set(page_rows)[:slot_count][:, None]  36.8 us
    scatter x1, local copies, waits for them, and re-layouts, shards(): send_rows = jnp.zeros((dest_count * capacity, PAGE, 2 * local_width), jnp...  22.5 us
    dot_general x1, matrix products, shards(): jnp.einsum('qhd,khd->hqk', queries.reshape(token_count, heads_here, HD),...  18.6 us
    reduce_sum x1, other arithmetic, shards(): totals = jnp.sum(weights, axis=2)  18.2 us
    unnamed x46, local copies, waits for them, and re-layouts  16.9 us
    reshape x1, local copies, waits for them, and re-layouts, join_heads(): split_rows.transpose(0, 2, 3, 1, 4)  16.6 us
    dot_general x1, matrix products, shards(): jnp.einsum('hqk,khd->qhd', prob_rows, values_all.reshape(-1, heads_here,...  15.3 us
  transfers between devices with their start and end apart: 11, of which 7 were waited for; matrix products, arithmetic and copies ran while one was open for 20% of the time, Pallas kernels for 0%

profile of v1, /device:TPU:1, one launch (start us, length us, event | category | flops | bytes accessed | tf_op | source)
XLA Modules:
  0.0 446.2 jit_solution(17304116291206696440)
XLA Ops:
  8.1 1.2 fusion.25
  9.2 13.5 %psum.7 = f32[512]{0:T(512)S(1)} all-reduce(f32[512]{0:T(512)S(1)} %fusion.25), channel_id=1, replica_groups=mesh['req'=16,'tp'=8] {'tp'}, use_global_device_ids=true, to_apply=%region_1.0 | all-reduce | flops 512 | bytes 4096 | tf_op jit(solution)/shard_map/psum | solution.py:121
  22.7 1.9 fusion.27
  24.6 2.9 collective-permute-start.4
  29.6 1.3 broadcast_compare_fusion
  30.9 1.6 pad_add_fusion
  32.6 2.5 collective-permute-start.1
  35.1 5.0 %collective-permute-done.1 = bf16[512,384]{1,0:T(8,128)(2,1)S(1)} collective-permute-done((bf16[512,384]{1,0:T(8,128)(2,1)}, bf16[512,384]{1,0:T(8,128)(2,1)S(1)}, u32[]{:S(2)}, u32[]{:S(2)}) %collective-permute-start.1) | collective-permute-done | bytes 393248 | tf_op jit(solution)/shard_map/ppermute | solution.py:28
  40.1 2.4 collective-permute-start.2
  42.8 2.9 collective-permute-start.5
  45.6 1.6 collective-permute-done.2
  47.2 2.6 collective-permute-start.3
  50.4 3.6 collective-permute-start.6
  57.1 1.1 constant_dynamic-update-slice_fusion.13
  58.2 1.1 constant_dynamic-update-slice_fusion.12
  59.6 1.1 constant_dynamic-update-slice_fusion.9
  63.1 1.2 constant_dynamic-update-slice_fusion.4
  64.6 1.1 constant_dynamic-update-slice_fusion.1
  65.8 2.6 fusion.15
  68.4 2.0 fusion.8
  70.4 2.0 fusion.6
  74.3 4.2 pad_maximum_fusion.2
  78.5 5.8 %copy.54 = bf16[4608,384]{0,1:T(8,128)(2,1)} copy(bf16[4608,384]{1,0:T(8,128)(2,1)} %pad_maximum_fusion.2) | data formatting | bytes 7077888 | tf_op jit(solution)/shard_map/concatenate | solution.py:139
  84.3 2.2 pad_maximum_fusion.1
  86.5 7.1 %pad_maximum_fusion = bf16[36,128,768]{2,1,0:T(8,128)(2,1)} fusion(bf16[36,128,384]{2,1,0:T(8,128)(2,1)S(1)} %bitcast.86, bf16[36,128,384]{2,1,0:T(8,128)(2,1)} %bitcast.87), kind=kLoop, calls=%fused_computation.13 | loop fusion | flops 14155776 | bytes 14155776 | tf_op jit(solution)/shard_map/concatenate | solution.py:167
  93.6 6.0 %broadcast_in_dim.20 = bf16[64,128,768]{2,1,0:T(8,128)(2,1)} broadcast(bf16[]{:T(256)} %constant.100.clone.1), dimensions={} | broadcast | bytes 12582914 | tf_op jit(solution)/shard_map/broadcast_in_dim | solution.py:190
  99.6 22.5 %scatter_fusion = bf16[64,128,768]{2,1,0:T(8,128)(2,1)} fusion(bf16[64,128,768]{2,1,0:T(8,128)(2,1)} %broadcast_in_dim.20, s32[36]{0:T(128)S(1)} %fusion.41, bf16[36,128,768]{2,1,0:T(8,128)(2,1)} %pad_maximum_fusion), kind=kCustom, calls=%fused_computation.1 | custom fusion | bytes 21233808 | tf_op jit(solution)/shard_map/scatter | solution.py:192
  122.1 7.8 %all-to-all-start.1 = ((bf16[64,128,768]{2,1,0:T(8,128)(2,1)}), bf16[64,128,768]{2,1,0:T(8,128)(2,1)}, u32[]{:S(2)}, u32[]{:S(2)}) async-start(bf16[64,128,768]{2,1,0:T(8,128)(2,1)} %scatter_fusion), calls=%async_computation.2 | async-start | bytes 25165824 | tf_op jit(solution)/shard_map/all_to_all | solution.py:196
  129.9 18.6 %fusion = (f32[4,512]{1,0:T(4,128)S(1)}, f32[4,512,4608]{2,1,0:T(8,128)}) fusion(pred[512,4608]{1,0:T(8,128)(4,1)} %pad_add_fusion, bf16[4608,4,96]{0,2,1:T(8,128)(2,1)} %bitcast.91, bf16[512,4,48]{0,2,1:T(8,128)(2,1)S(1)} %copy-done.9, bf16[512,4,48]{0,2,1:T(8,128)(2,1)S(1)} %copy-done.8), kind=kOutput, calls=%fused_computation.5 | convolution fusion | flops 1841035264 | bytes 44048384 | tf_op jit(solution)/shard_map/qhd,khd->hqk/dot_general | solution.py:143
  148.5 5.7 %copy.52 = bf16[4608,384]{0,1:T(8,128)(2,1)} copy(bf16[4608,384]{1,0:T(8,128)(2,1)} %copy-done.1) | data formatting | bytes 7077888 | tf_op jit(solution)/shard_map/concatenate | solution.py:140
  154.2 18.2 %fusion.1 = f32[4,512]{1,0:T(4,128)S(1)} fusion(f32[4,512,4608]{2,1,0:T(8,128)} %get-tuple-element.26, f32[4,512]{1,0:T(4,128)S(1)} %get-tuple-element.25, pred[512,4608]{1,0:T(8,128)(4,1)} %pad_add_fusion), kind=kLoop, calls=%fused_computation.6 | loop fusion | flops 37746688 | bytes 40124416 | tf_op jit(solution)/shard_map/reduce_sum | solution.py:152
  172.5 15.3 %fusion.21 = bf16[512,4,96]{0,2,1:T(8,128)(2,1)S(1)} fusion(bf16[4608,4,96]{0,2,1:T(8,128)(2,1)S(1)} %bitcast.92, f32[4,512,4608]{2,1,0:T(8,128)} %get-tuple-element.26, f32[4,512]{1,0:T(4,128)S(1)} %get-tuple-element.25, pred[512,4608]{1,0:T(8,128)(4,1)S(1)} %copy-done.3, f32[512,4]{0,1:T(4,128)S(1)} %bitcast.97), kind=kOutput, calls=%fused_computation.31 | convolution fusion | flops 1850081280 | bytes 44056576 | tf_op jit(solution)/shard_map/hqk,khd->qhd/dot_general | solution.py:154
  187.8 4.5 %fusion.49 = f32[512,3072]{1,0:T(8,128)} fusion(bf16[512,384]{0,1:T(8,128)(2,1)S(1)} %bitcast.96, bf16[384,3072]{1,0:T(8,128)(2,1)S(1)} %copy-done), kind=kOutput, calls=%fused_computation.106 | convolution fusion | flops 1207959552 | bytes 9043968 | tf_op jit(solution)/shard_map/dot_general | solution.py:163
  192.4 108.1 %all-to-all-done.1 = bf16[64,128,768]{2,1,0:T(8,128)(2,1)} async-done(((bf16[64,128,768]{2,1,0:T(8,128)(2,1)}), bf16[64,128,768]{2,1,0:T(8,128)(2,1)}, u32[]{:S(2)}, u32[]{:S(2)}) %all-to-all-start.1) | async-done | bytes 12582944 | tf_op jit(solution)/shard_map/all_to_all | solution.py:196
  300.5 10.7 %constant_dynamic-slice_fusion.1 = (bf16[16,1,2,128,768]{4,3,2,1,0:T(8,128)(2,1)}, bf16[16,1,2,128,768]{4,3,2,1,0:T(8,128)(2,1)}) fusion(bf16[16,2,2,128,768]{4,3,2,1,0:T(8,128)(2,1)} %bitcast.28, s32[]{:T(128)S(6)} %select_n.100, s32[]{:T(128)S(6)} %select_n.103), kind=kLoop, calls=%fused_computation.86 | loop fusion | bytes 25165832 | tf_op jit(solution)/shard_map/jit(dynamic_index_in_dim)/dynamic_slice | solution.py:201
  311.1 8.5 %collective-permute-start.7 = (bf16[32,128,768]{2,1,0:T(8,128)(2,1)}, bf16[32,128,768]{2,1,0:T(8,128)(2,1)}, u32[]{:S(2)}, u32[]{:S(2)}) collective-permute-start(bf16[32,128,768]{2,1,0:T(8,128)(2,1)} %bitcast.90), channel_id=1, source_target_pairs={{0,1},{1,0},{2,3},{3,2},{4,5},{5,4},{6,7},{7,6},{8,9},{9,8},{10,11... | collective-permute-start | bytes 18874376 | tf_op jit(solution)/shard_map/ppermute | solution.py:43
  321.0 6.5 %all-to-all-start = ((s32[16,4,1]{1,2,0:T(1,128)}), s32[16,4,1]{1,2,0:T(1,128)S(1)}, u32[]{:S(2)}, u32[]{:S(2)}) async-start(s32[16,4,1]{1,2,0:T(1,128)} %bitcast.23), calls=%async_computation.1 | async-start | bytes 16384 | tf_op jit(solution)/shard_map/all_to_all | solution.py:197
  327.6 6.3 %all-to-all-done = s32[16,4,1]{1,2,0:T(1,128)S(1)} async-done(((s32[16,4,1]{1,2,0:T(1,128)}), s32[16,4,1]{1,2,0:T(1,128)S(1)}, u32[]{:S(2)}, u32[]{:S(2)}) %all-to-all-start) | async-done | bytes 288 | tf_op jit(solution)/shard_map/all_to_all | solution.py:197
  334.2 2.0 fusion.28
  336.1 10.3 %bitcast_select_fusion.1 = (bf16[32,128,768]{2,1,0:T(8,128)(2,1)}, bf16[32,128,768]{2,1,0:T(8,128)(2,1)}) fusion(bf16[32,128,768]{2,1,0:T(8,128)(2,1)} %collective-permute-done.7, bf16[16,1,2,128,768]{4,3,2,1,0:T(8,128)(2,1)} %get-tuple-element.14, pred[]{:T(512)S(6)} %eq.78), kind=kLoop, calls=%fused_computation.15 | loop fusion | flops 6291456 | bytes 25165824 | tf_op jit(solution)/shard_map/jit(_where)/select_n | solution.py:89
  346.5 8.7 %copy.58 = bf16[32,128,768]{1,2,0:T(8,128)(2,1)} copy(bf16[32,128,768]{2,1,0:T(8,128)(2,1)} %get-tuple-element.12) | data formatting | bytes 12582912 | tf_op jit(solution)/shard_map/jit(_where)/select_n | solution.py:89
  355.2 8.6 %copy.59 = bf16[32,128,768]{1,2,0:T(8,128)(2,1)} copy(bf16[32,128,768]{2,1,0:T(8,128)(2,1)} %get-tuple-element.13) | data formatting | bytes 12582912 | tf_op jit(solution)/shard_map/jit(_where)/select_n | solution.py:90
  363.8 6.2 %maximum_bitcast_fusion = bf16[32,128,2,2,384]{1,4,2,0,3:T(8,128)(2,1)S(1)} fusion(bf16[32,1,128,2,384]{2,4,3,0,1:T(8,128)(2,1)} %bitcast.89, bf16[32,1,128,2,384]{2,4,3,0,1:T(8,128)(2,1)} %bitcast.88), kind=kLoop, calls=%fused_computation.10 | loop fusion | flops 6291456 | bytes 25165824 | tf_op jit(solution)/shard_map/transpose | solution.py:97
  369.9 5.7 %copy.60 = bf16[32,128,2,2,384]{1,4,3,2,0:T(8,128)(2,1)} copy(bf16[32,128,2,2,384]{1,4,2,0,3:T(8,128)(2,1)S(1)} %maximum_bitcast_fusion) | data formatting | bytes 25165824 | tf_op jit(solution)/shard_map/transpose | solution.py:97
  375.7 16.6 %copy.61 = bf16[32,128,1536]{2,1,0:T(8,128)(2,1)} copy(bf16[32,128,1536]{1,2,0:T(8,128)(2,1)} %bitcast.85) | data formatting | bytes 25165824 | tf_op jit(solution)/shard_map/reshape | solution.py:97
  392.3 3.7 broadcast_in_dim.18
  396.0 36.8 %scatter_fusion.1 = bf16[19,128,1536]{2,1,0:T(8,128)(2,1)} fusion(bf16[19,128,1536]{2,1,0:T(8,128)(2,1)} %broadcast_in_dim.18, s32[32]{0:T(128)S(1)} %fusion.42, bf16[32,128,1536]{2,1,0:T(8,128)(2,1)} %copy.61), kind=kCustom, calls=%fused_computation.2 | custom fusion | bytes 37748864 | tf_op jit(solution)/shard_map/scatter | solution.py:102
  432.8 6.6 %slice_bitcast_fusion = bf16[18,1,128,1536]{3,2,1,0:T(8,128)(2,1)} fusion(bf16[19,128,1536]{2,1,0:T(8,128)(2,1)} %scatter_fusion.1), kind=kLoop, calls=%fused_computation.12 | loop fusion | bytes 14155776
  (79 shorter events, 13.7 us)
Async XLA Ops:
  7.2 180.6 %copy-start = (bf16[384,3072]{1,0:T(8,128)(2,1)S(1)}, bf16[384,3072]{1,0:T(8,128)(2,1)}, u32[]{:S(2)}) copy-start(bf16[384,3072]{1,0:T(8,128)(2,1)} %param.16) | copy-start | bytes 7077892
  7.2 52.1 %copy-start.2 = (bf16[512,384]{1,0:T(8,128)(2,1)S(1)}, bf16[512,384]{1,0:T(8,128)(2,1)}, u32[]{:S(2)}) copy-start(bf16[512,384]{1,0:T(8,128)(2,1)} %param.11) | copy-start | bytes 1179652
  7.2 25.3 %copy-start.15 = (s32[1,4]{1,0:T(1,128)S(1)}, s32[1,4]{1,0:T(1,128)}, u32[]{:S(2)}) copy-start(s32[1,4]{1,0:T(1,128)} %param.20) | copy-start | bytes 52
  7.2 35.4 %copy-start.11 = (s32[1,4]{1,0:T(1,128)S(1)}, s32[1,4]{1,0:T(1,128)}, u32[]{:S(2)}) copy-start(s32[1,4]{1,0:T(1,128)} %param.19) | copy-start | bytes 52
  7.2 27.8 %copy-start.10 = (s32[1,36]{1,0:T(1,128)S(1)}, s32[1,36]{1,0:T(1,128)}, u32[]{:S(2)}) copy-start(s32[1,36]{1,0:T(1,128)} %param.21) | copy-start | bytes 436
  24.6 18.1 %collective-permute-start.4 = (bf16[512,384]{1,0:T(8,128)(2,1)}, bf16[512,384]{1,0:T(8,128)(2,1)S(1)}, u32[]{:S(2)}, u32[]{:S(2)}) collective-permute-start(bf16[512,384]{1,0:T(8,128)(2,1)} %fusion.27), channel_id=1, source_target_pairs={{0,7},{1,0},{2,1},{3,2},{4,3},{5,4},{6,5},{7,6},{8,15},{9,8},{10,9... | collective-permute-start | bytes 1179656 | tf_op jit(solution)/shard_map/ppermute | solution.py:32
  27.5 5.0 %collective-permute-start = (bf16[512,384]{1,0:T(8,128)(2,1)}, bf16[512,384]{1,0:T(8,128)(2,1)}, u32[]{:S(2)}, u32[]{:S(2)}) collective-permute-start(bf16[512,384]{1,0:T(8,128)(2,1)} %fusion.27), channel_id=1, source_target_pairs={{0,1},{1,2},{2,3},{3,4},{4,5},{5,6},{6,7},{7,0},{8,9},{9,10},{10,1... | collective-permute-start | bytes 1179656 | tf_op jit(solution)/shard_map/ppermute | solution.py:28
  32.6 7.5 %collective-permute-start.1 = (bf16[512,384]{1,0:T(8,128)(2,1)}, bf16[512,384]{1,0:T(8,128)(2,1)S(1)}, u32[]{:S(2)}, u32[]{:S(2)}) collective-permute-start(bf16[512,384]{1,0:T(8,128)(2,1)} %collective-permute-done), channel_id=1, source_target_pairs={{0,1},{1,2},{2,3},{3,4},{4,5},{5,6},{6,7},{7,0},{8,9},{9,10},{10,1... | collective-permute-start | bytes 1179656 | tf_op jit(solution)/shard_map/ppermute | solution.py:28
  40.1 2.7 copy-start.5
  40.1 7.1 %collective-permute-start.2 = (bf16[512,384]{1,0:T(8,128)(2,1)S(1)}, bf16[512,384]{1,0:T(8,128)(2,1)}, u32[]{:S(2)}, u32[]{:S(2)}) collective-permute-start(bf16[512,384]{1,0:T(8,128)(2,1)S(1)} %collective-permute-done.1), channel_id=1, source_target_pairs={{0,1},{1,2},{2,3},{3,4},{4,5},{5,6},{6,7},{7,0},{8,9},{9,10},{10,1... | collective-permute-start | bytes 1179656 | tf_op jit(solution)/shard_map/ppermute | solution.py:28
  42.8 7.6 %collective-permute-start.5 = (bf16[512,384]{1,0:T(8,128)(2,1)S(1)}, bf16[512,384]{1,0:T(8,128)(2,1)}, u32[]{:S(2)}, u32[]{:S(2)}) collective-permute-start(bf16[512,384]{1,0:T(8,128)(2,1)S(1)} %collective-permute-done.4), channel_id=1, source_target_pairs={{0,7},{1,0},{2,1},{3,2},{4,3},{5,4},{6,5},{7,6},{8,15},{9,8},{10,9... | collective-permute-start | bytes 1179656 | tf_op jit(solution)/shard_map/ppermute | solution.py:32
  47.2 7.8 %collective-permute-start.3 = (bf16[512,384]{1,0:T(8,128)(2,1)}, bf16[512,384]{1,0:T(8,128)(2,1)}, u32[]{:S(2)}, u32[]{:S(2)}) collective-permute-start(bf16[512,384]{1,0:T(8,128)(2,1)} %collective-permute-done.2), channel_id=1, source_target_pairs={{0,1},{1,2},{2,3},{3,4},{4,5},{5,6},{6,7},{7,0},{8,9},{9,10},{10,1... | collective-permute-start | bytes 1179656 | tf_op jit(solution)/shard_map/ppermute | solution.py:28
  49.8 13.2 %copy-start.6 = (bf16[512,384]{1,0:T(8,128)(2,1)S(1)}, bf16[512,384]{1,0:T(8,128)(2,1)}, u32[]{:S(2)}) copy-start(bf16[512,384]{1,0:T(8,128)(2,1)} %copy-done.5) | copy-start | bytes 1179652
  50.3 15.6 %copy-start.12 = (bf16[3072,384]{1,0:T(8,128)(2,1)S(1)}, bf16[3072,384]{1,0:T(8,128)(2,1)}, u32[]{:S(2)}) copy-start(bf16[3072,384]{1,0:T(8,128)(2,1)} %param.15) | copy-start | bytes 7077892
  50.4 10.3 %collective-permute-start.6 = (bf16[512,384]{1,0:T(8,128)(2,1)}, bf16[512,384]{1,0:T(8,128)(2,1)S(1)}, u32[]{:S(2)}, u32[]{:S(2)}) collective-permute-start(bf16[512,384]{1,0:T(8,128)(2,1)} %collective-permute-done.5), channel_id=1, source_target_pairs={{0,7},{1,0},{2,1},{3,2},{4,3},{5,4},{6,5},{7,6},{8,15},{9,8},{10,9... | collective-permute-start | bytes 1179656 | tf_op jit(solution)/shard_map/ppermute | solution.py:32
  63.1 5.4 %copy-start.13 = (bf16[3072,384]{1,0:T(8,128)(2,1)S(1)}, bf16[3072,384]{1,0:T(8,128)(2,1)}, u32[]{:S(2)}) copy-start(bf16[3072,384]{1,0:T(8,128)(2,1)} %param.13) | copy-start | bytes 7077892
  68.4 2.0 copy-start.14
  74.3 9.9 %copy-start.7 = (bf16[512,384]{1,0:T(8,128)(2,1)S(1)}, bf16[512,384]{1,0:T(8,128)(2,1)}, u32[]{:S(2)}) copy-start(bf16[512,384]{1,0:T(8,128)(2,1)} %fusion.15) | copy-start | bytes 1179652
  86.5 7.1 %copy-start.1 = (bf16[4608,384]{1,0:T(8,128)(2,1)}, bf16[4608,384]{1,0:T(8,128)(2,1)S(1)}, u32[]{:S(2)}) copy-start(bf16[4608,384]{1,0:T(8,128)(2,1)S(1)} %pad_maximum_fusion.1) | copy-start | bytes 10616836
  122.1 7.8 %copy-start.8 = (bf16[512,4,48]{0,2,1:T(8,128)(2,1)S(1)}, bf16[512,4,48]{0,2,1:T(8,128)(2,1)}, u32[]{:S(2)}) copy-start(bf16[512,4,48]{0,2,1:T(8,128)(2,1)} %get-tuple-element.16) | copy-start | bytes 589828
  122.1 7.8 %copy-start.9 = (bf16[512,4,48]{0,2,1:T(8,128)(2,1)S(1)}, bf16[512,4,48]{0,2,1:T(8,128)(2,1)}, u32[]{:S(2)}) copy-start(bf16[512,4,48]{0,2,1:T(8,128)(2,1)} %get-tuple-element.17) | copy-start | bytes 589828
  122.1 178.4 %all-to-all-start.1 = ((bf16[64,128,768]{2,1,0:T(8,128)(2,1)}), bf16[64,128,768]{2,1,0:T(8,128)(2,1)}, u32[]{:S(2)}, u32[]{:S(2)}) async-start(bf16[64,128,768]{2,1,0:T(8,128)(2,1)} %scatter_fusion), calls=%async_computation.2 | async-start | bytes 25165824 | tf_op jit(solution)/shard_map/all_to_all | solution.py:196
  129.8 204.3 %reduce-scatter.2.cloned.1.call-start = ((), (), s32[]{:S(2)}) async-start(), calls=%async_computation.3 | async-start | bytes 7077888 | tf_op jit(solution)/shard_map/reduce_scatter | solution.py:164
  154.2 18.2 %copy-start.3 = (pred[512,4608]{1,0:T(8,128)(4,1)S(1)}, pred[512,4608]{1,0:T(8,128)(4,1)}, u32[]{:S(2)}) copy-start(pred[512,4608]{1,0:T(8,128)(4,1)} %pad_add_fusion) | copy-start | bytes 7077892
  154.2 18.2 %copy-start.4 = (bf16[4608,384]{0,1:T(8,128)(2,1)S(1)}, bf16[4608,384]{0,1:T(8,128)(2,1)}, u32[]{:S(2)}) copy-start(bf16[4608,384]{0,1:T(8,128)(2,1)} %copy.52) | copy-start | bytes 10616836
  311.1 25.0 %collective-permute-start.7 = (bf16[32,128,768]{2,1,0:T(8,128)(2,1)}, bf16[32,128,768]{2,1,0:T(8,128)(2,1)}, u32[]{:S(2)}, u32[]{:S(2)}) collective-permute-start(bf16[32,128,768]{2,1,0:T(8,128)(2,1)} %bitcast.90), channel_id=1, source_target_pairs={{0,1},{1,0},{2,3},{3,2},{4,5},{5,4},{6,7},{7,6},{8,9},{9,8},{10,11... | collective-permute-start | bytes 18874376 | tf_op jit(solution)/shard_map/ppermute | solution.py:43
  321.0 12.8 %all-to-all-start = ((s32[16,4,1]{1,2,0:T(1,128)}), s32[16,4,1]{1,2,0:T(1,128)S(1)}, u32[]{:S(2)}, u32[]{:S(2)}) async-start(s32[16,4,1]{1,2,0:T(1,128)} %bitcast.23), calls=%async_computation.1 | async-start | bytes 16384 | tf_op jit(solution)/shard_map/all_to_all | solution.py:197
Sparse Core Ops, SparseCore 0:
  192.5 47.8 reduce-scatter.1
